TPU v7x, 512 devices: a whole 4x8x8 slice. The times are simulated.
512 devices in a mesh: segment: 16 (over z, core), mp: 32 (over y, x).
Axes of the slice: x: 4, y: 8, z: 8, core: 2. Of those that a mesh axis runs over, the one named last changes fastest.
Arguments:
- rows: bfloat16 [16, 2, 128, 8192], P('segment', None, None, 'mp'), may hold values from -6 to 6
- carry: bfloat16 [16, 128, 8192], P('segment', None, 'mp'), may hold values from -6 to 6
- weights: bfloat16 [16, 2, 8192, 4096], P('segment', None, None, 'mp'), may hold values from -1.1932427 to 1.1932427
- neighbours: int32 [16, 2, 2, 2], P('segment'), may hold values from 0 to 7, all different within a row
Outputs:
- passed: bfloat16 [16, 128, 8192], P('segment', None, 'mp')
- returned: bfloat16 [16, 128, 8192], P('segment', None, 'mp')
- kv_grad: bfloat16 [1024, 2, 4096], P(None, None, 'mp')
Inputs may be any that keep to these rules, and one draw needn't show every extreme that they name: Each group's 2 neighbours are different pool blocks; pool blocks are numbered by encoder segment in order, then by row.
All inputs are finite; a program needn't handle non-finite values.
Results may differ from a plain program's by a relative error of at most 0.02.
The roundings to bfloat16 on the way count: a program that leaves them out, or rounds other values in their place, can miss the bound.
Values may be sent and summed in bfloat16 or wider, within the bound.
No kernel may reach another device: no remote copies, remote signals or barrier semaphores. Data moves between devices by JAX's collectives and lax.ppermute only.
A program may use at most 64 MiB of HBM per device.

v0:
```python
import functools
import math
import numpy as np
import jax
import jax.numpy as jnp
from jax import lax
from jax.sharding import Mesh, PartitionSpec as P

GROUP = 64
NBLEN = 128
NEIGH = 2


def from_behind(x, axis, by):
    devices = lax.axis_size(axis)
    return lax.ppermute(x, axis, [(i, (i + by) % devices) for i in range(devices)])


def attend(queries, key_rows, score_scale):
    scores = (
        jnp.einsum("cqd,ckd->cqk", queries, key_rows, preferred_element_type=jnp.float32)
        * score_scale
    )
    soft = jax.nn.softmax(scores, axis=-1)
    return (soft, soft.astype(jnp.bfloat16))


def attend_back(queries, key_rows, value_rows, soft, rounded, upstream, score_scale):
    d_soft = jnp.einsum("cqd,ckd->cqk", upstream, value_rows, preferred_element_type=jnp.float32)
    grad_values = jnp.einsum("cqk,cqd->ckd", rounded, upstream, preferred_element_type=jnp.float32)
    d_scores = soft * (d_soft - jnp.sum(d_soft * soft, axis=-1, keepdims=True))
    grad_queries = (
        jnp.einsum("cqk,ckd->cqd", d_scores, key_rows.astype(jnp.float32)) * score_scale
    ).astype(jnp.bfloat16)
    grad_keys = jnp.einsum("cqk,cqd->ckd", d_scores, queries.astype(jnp.float32)) * score_scale
    return (grad_queries, grad_keys, grad_values)


def head_sum(terms, axis, tie):
    count, width, tokens = terms.shape
    rounded = terms.astype(jnp.bfloat16)
    if isinstance(axis, tuple):
        tall, wide = (lax.axis_size(axis[0]), lax.axis_size(axis[1]))
        parts = rounded.reshape(count, tall, wide, width // (tall * wide), tokens).transpose(
            1, 2, 0, 3, 4
        )
        partial = lax.psum_scatter(parts, axis[0], scatter_dimension=0, tiled=True)[0]
        partial, tie = lax.optimization_barrier((partial, tie))
        moved = lax.all_to_all(partial, axis[1], 0, 0, tiled=True)
        summed = jnp.sum(moved.astype(jnp.float32), axis=0)
    else:
        devices = lax.axis_size(axis)
        parts = rounded.reshape(count, devices, width // devices, tokens).transpose(1, 0, 2, 3)
        moved = lax.all_to_all(parts, axis, 0, 0, tiled=True)
        summed = jnp.sum(moved.astype(jnp.float32), axis=0)
    return (summed.transpose(0, 2, 1), tie)


def segment_sum(contrib, axis):
    devices = lax.axis_size(axis)
    parts = contrib.reshape(devices, contrib.shape[0] // devices, contrib.shape[1])
    moved = lax.all_to_all(parts, axis, 0, 0, tiled=True)
    summed = jnp.sum(moved.astype(jnp.float32), axis=0).astype(jnp.bfloat16)
    spread = jnp.broadcast_to(summed[None], (devices,) + summed.shape)
    return lax.all_to_all(spread, axis, 0, 0, tiled=True).reshape(contrib.shape)


def per_device(mp, stages, rows, carry, weights, neighbours):
    seg = ("sg", "sr")
    segments = lax.axis_size(seg)
    encoders = lax.axis_size("sr")
    first_encoder = segments - encoders
    last_group = lax.axis_size("sg") - 1
    group = lax.axis_index("sg")
    is_encoder = group == last_group
    local_rows = rows[0]
    local_carry = carry[0]
    gathered = jnp.concatenate([local_rows, local_carry[None]], axis=0)
    for stage in stages:
        gathered = lax.all_gather(gathered, stage, axis=2, tiled=True)
    full_rows, full_carry = (gathered[:2], gathered[2])
    tokens = local_rows.shape[1]
    width = full_rows.shape[2]
    head = weights.shape[3]
    w_query = weights[0, 0]
    w_out = weights[0, 1]

    def encode():
        flat = full_rows.reshape(2 * tokens, width)
        keyval = jnp.concatenate(
            [
                jnp.dot(flat, w_query, preferred_element_type=jnp.float32),
                jnp.dot(flat, w_out, preferred_element_type=jnp.float32),
            ],
            axis=-1,
        ).astype(jnp.bfloat16)
        return (keyval, jnp.zeros((2 * tokens, head), jnp.bfloat16))

    def decode():
        queries = jnp.dot(
            full_rows.reshape(2 * tokens, width), w_query, preferred_element_type=jnp.float32
        ).astype(jnp.bfloat16)
        return (jnp.zeros((2 * tokens, 2 * head), jnp.bfloat16), queries)

    encoded, queries = lax.cond(is_encoder, encode, decode)
    per_encoder = 2 * tokens // NBLEN
    pool_blocks = encoders * per_encoder
    piece = encoded
    for target in range(last_group):
        arrived = lax.ppermute(encoded, "sg", [(last_group, target)])
        piece = jnp.where(group == target, arrived, piece)
    pool = lax.all_gather(piece, "sr", axis=0, tiled=True).reshape(pool_blocks, NBLEN, 2 * head)
    groups = tokens // GROUP
    local_nbr = neighbours[0]
    score_scale = 1.0 / math.sqrt(head)
    query_blocks = queries.reshape(2, groups, GROUP, head)

    def fetch(batch):
        picked = pool[local_nbr[batch]].reshape(groups, NEIGH * NBLEN, 2 * head)
        return (picked[..., :head], picked[..., head:])

    keys_fwd, values_fwd = fetch(0)
    soft_fwd, rounded_fwd = attend(query_blocks[0], keys_fwd, score_scale)
    mixed = jnp.einsum(
        "cqk,ckd->cqd", rounded_fwd, values_fwd, preferred_element_type=jnp.float32
    ).astype(jnp.bfloat16)
    mixed_flat = mixed.reshape(tokens, head)
    upstream = (
        jnp.dot(full_carry, w_out, preferred_element_type=jnp.float32)
        .astype(jnp.bfloat16)
        .reshape(groups, GROUP, head)
    )
    keys_back, values_back = fetch(1)
    soft_back, rounded_back = attend(query_blocks[1], keys_back, score_scale)
    grad_queries, grad_keys, grad_values = attend_back(
        query_blocks[1], keys_back, values_back, soft_back, rounded_back, upstream, score_scale
    )
    grad_flat = grad_queries.reshape(tokens, head)
    terms = jnp.stack(
        [
            lax.dot_general(
                w_out, mixed_flat, (((1,), (1,)), ((), ())), preferred_element_type=jnp.float32
            ),
            lax.dot_general(
                w_query, grad_flat, (((1,), (1,)), ((), ())), preferred_element_type=jnp.float32
            ),
        ]
    )
    onehot = (
        local_nbr[1][..., None] == jnp.arange(pool_blocks, dtype=jnp.int32)[None, None, :]
    ).astype(jnp.float32)
    grad_keyval = jnp.concatenate([grad_keys, grad_values], axis=-1).reshape(
        groups, NEIGH, NBLEN, 2 * head
    )
    contrib = jnp.einsum("cbp,cbrf->prf", onehot, grad_keyval)
    contrib = jnp.where(is_encoder, jnp.zeros_like(contrib), contrib)
    pooled = segment_sum(contrib.astype(jnp.bfloat16).reshape(pool_blocks * NBLEN, 2 * head), seg)
    kv_grad = pooled.reshape(pool_blocks * NBLEN, 2, head)
    summed, kv_grad = head_sum(terms, mp, kv_grad)
    out_sum, grad_input = summed
    forward_rows = (local_rows[0].astype(jnp.float32) + out_sum).astype(jnp.bfloat16)
    forward_rows = jnp.where(is_encoder, local_carry, forward_rows)
    passed = from_behind(forward_rows[None], seg, 1)
    back = local_carry.astype(jnp.float32) + grad_input
    back_rows = jnp.where(is_encoder, local_carry, back.astype(jnp.bfloat16))
    returned = from_behind(back_rows[None], seg, -1)
    return (passed, returned, kv_grad)


def split_mesh(mesh):
    devices = mesh.devices
    segments = devices.shape[0]
    encoders = segments // 4
    groups = segments // encoders
    try:
        xs = [d.coords[0] for d in devices[0]]
        ys = [d.coords[1] for d in devices[0]]
        wide = len(set(xs))
        tall = devices.shape[1] // wide
        grid_x = np.array(xs).reshape(tall, wide)
        grid_y = np.array(ys).reshape(tall, wide)
        ok = (
            wide * tall == devices.shape[1]
            and wide > 1
            and (tall > 1)
            and (grid_x == grid_x[:1]).all()
            and (grid_y == grid_y[:, :1]).all()
        )
    except (AttributeError, TypeError, IndexError, ValueError):
        ok = False
    if ok:
        view = devices.reshape(groups, encoders, tall, wide)
        return (Mesh(view, ("sg", "sr", "my", "mx")), ("my", "mx"), ("mx", "my"))
    view = devices.reshape(groups, encoders, devices.shape[1])
    return (Mesh(view, ("sg", "sr", "mp")), "mp", ("mp",))


def solution(mesh):
    inner, mp, stages = split_mesh(mesh)
    seg = ("sg", "sr")
    placed = (
        P(seg, None, None, mp),
        P(seg, None, mp),
        P(seg, None, None, mp),
        P(seg, None, None, None),
    )
    return jax.shard_map(
        functools.partial(per_device, mp, stages),
        mesh=inner,
        in_specs=placed,
        out_specs=(P(seg, None, mp), P(seg, None, mp), P(None, None, mp)),
        check_vma=False,
    )
```

profile of v0, /device:TPU:24, one launch (start us, length us, event | category | flops | bytes accessed | tf_op | source)
XLA Modules:
  0.0 234.3 jit_solution(7432874130987226434)
XLA Ops:
  7.2 0.0 copy-start.3
  7.2 0.0 all-gather.2.cloned.1.call-start
  7.2 1.0 pad_maximum_fusion.2
  8.2 14.4 %all_gather.9 = bf16[3,128,1024]{2,1,0:T(8,128)(2,1)} all-gather(bf16[3,128,256]{2,1,0:T(8,128)(2,1)S(1)} %pad_maximum_fusion.2), channel_id=1, replica_groups=mesh['sg'=4,'sr'=4,'my'=8,'mx'=4] {'mx'}, dimensions={2}, use_global_device_ids=true | all-gather | bytes 983040 | tf_op jit(solution)/shard_map/all_gather | solution.py:80
  22.6 0.0 all-gather.2.cloned.1.call-update
  22.6 0.0 reduce-scatter.2.cloned.1.call-start
  22.7 0.0 copy-done.3
  22.7 0.1 reshape.139
  22.8 0.1 reshape.147
  22.9 3.8 %slice_bitcast_fusion.2 = (bf16[8192,128]{1,0:T(8,128)(2,1)}, bf16[8192,128]{1,0:T(8,128)(2,1)S(1)}) fusion(bf16[1,2,8192,128]{3,2,1,0:T(8,128)(2,1)} %param.8), kind=kLoop, calls=%fused_computation.15 | loop fusion | bytes 8388608 | tf_op jit(solution)/shard_map/squeeze | solution.py:86
  26.7 77.2 %all-gather.2.cloned.1.call-done = bf16[3,128,8192]{2,1,0:T(8,128)(2,1)} async-done(((bf16[3,128,1024]{2,1,0:T(8,128)(2,1)}), bf16[3,128,8192]{2,1,0:T(8,128)(2,1)}) %all-gather.2.cloned.1.call-update) | async-done | bytes 6291472 | tf_op jit(solution)/shard_map/all_gather | solution.py:80
  103.9 0.0 slice-start
  103.9 0.0 copy-start
  103.9 2.2 slice-done
  106.1 0.7 copy-done
  106.7 1.3 conditional.1
  106.7 1.3 convolution_convert_fusion
  108.1 1.3 collective-permute-start.2
  109.4 0.7 collective-permute-start.1
  110.1 0.7 collective-permute-start
  110.7 2.9 %fusion.12 = bf16[128,128]{1,0:T(8,128)(2,1)S(1)} fusion(bf16[3,128,8192]{2,1,0:T(8,128)(2,1)} %all-gather.2.cloned.1.call-done, bf16[1,2,8192,128]{3,2,1,0:T(8,128)(2,1)} %param.8), kind=kOutput, calls=%fused_computation.29 | convolution fusion | flops 268451840 | bytes 4227072 | tf_op jit(solution)/shard_map/dot_general | solution.py:129
  113.7 6.7 %collective-permute-done.2 = bf16[256,256]{1,0:T(8,128)(2,1)S(1)} collective-permute-done((bf16[256,256]{1,0:T(8,128)(2,1)S(1)}, bf16[256,256]{1,0:T(8,128)(2,1)S(1)}, u32[]{:S(2)}, u32[]{:S(2)}) %collective-permute-start.2) | collective-permute-done | bytes 131104 | tf_op jit(solution)/shard_map/ppermute | solution.py:110
  120.4 0.0 collective-permute-done.1
  120.4 0.0 collective-permute-done
  120.4 11.1 %all_gather.11 = bf16[1024,256]{1,0:T(8,128)(2,1)S(1)} all-gather(bf16[256,256]{1,0:T(8,128)(2,1)S(1)} %select_select_fusion), channel_id=1, replica_groups=mesh['sg'=4,'sr'=4,'my'=8,'mx'=4] {'sr'}, dimensions={0}, use_global_device_ids=true | all-gather | bytes 655360 | tf_op jit(solution)/shard_map/all_gather | solution.py:112
  131.5 0.6 gather_fusion.1
  132.1 0.6 gather_fusion
  132.7 0.2 convolution_multiply_fusion.2
  132.8 0.2 fusion.33
  133.0 0.3 convolution_convert_fusion.5
  133.3 0.2 convolution_multiply_fusion.1
  133.5 0.4 fusion.32
  133.9 0.3 multiply_reduce_fusion
  134.1 0.3 fusion.11
  134.5 2.3 fusion.3
  136.8 2.5 %copy.23 = bf16[8192,128]{1,0:T(8,128)(2,1)} copy(bf16[8192,128]{0,1:T(8,128)(2,1)S(1)} %fusion.3) | data formatting | bytes 4194304 | tf_op jit(solution)/shard_map/stack | solution.py:139
  139.3 2.3 fusion.2
  141.6 2.5 %copy.22 = bf16[8192,128]{1,0:T(8,128)(2,1)} copy(bf16[8192,128]{0,1:T(8,128)(2,1)S(1)} %fusion.2) | data formatting | bytes 4194304 | tf_op jit(solution)/shard_map/stack | solution.py:139
  144.0 4.5 %maximum_bitcast_fusion = bf16[8,4,2,256,128]{4,3,2,1,0:T(8,128)(2,1)} fusion(bf16[1,8,4,256,128]{4,3,0,2,1:T(8,128)(2,1)} %bitcast.82, bf16[1,8,4,256,128]{4,3,0,2,1:T(8,128)(2,1)} %bitcast.83), kind=kLoop, calls=%fused_computation.12 | loop fusion | flops 2097152 | bytes 8388608 | tf_op jit(solution)/shard_map/transpose | solution.py:44
  148.6 0.0 reduce-scatter.2.cloned.1.call-update
  148.6 0.1 copy.17
  148.7 0.3 fusion.23
  149.0 0.4 convolution_multiply_fusion
  149.4 0.1 reshape.135
  149.5 0.5 copy.18
  150.0 0.5 fusion.6
  150.5 0.1 copy.19
  150.6 21.9 %all_to_all.15 = bf16[16,64,256]{2,1,0:T(8,128)(2,1)S(1)} all-to-all(bf16[16,64,256]{2,1,0:T(8,128)(2,1)S(1)} %bitcast.86), channel_id=1, replica_groups=mesh['sg'=4,'sr'=4,'my'=8,'mx'=4] {'sg','sr'}, dimensions={0} | all-to-all | bytes 1048576 | tf_op jit(solution)/shard_map/all_to_all | solution.py:62
  172.6 0.1 reduce_sum.51
  172.7 20.0 %all_to_all.16 = bf16[16,64,256]{2,1,0:T(8,128)(2,1)S(1)} all-to-all(bf16[16,64,256]{2,1,0:T(8,128)(2,1)S(1)} %broadcast_in_dim.5), channel_id=1, replica_groups=mesh['sg'=4,'sr'=4,'my'=8,'mx'=4] {'sg','sr'}, dimensions={0} | all-to-all | bytes 1048576 | tf_op jit(solution)/shard_map/all_to_all | solution.py:65
  192.7 0.0 copy-start.1
  192.7 0.9 reshape_reshape.7
  193.6 10.4 %reduce-scatter.2.cloned.1.call-done = bf16[1,4,2,256,128]{4,3,2,1,0:T(8,128)(2,1)} async-done(((bf16[8,4,2,256,128]{4,3,2,1,0:T(8,128)(2,1)}), bf16[1,4,2,256,128]{4,3,2,1,0:T(8,128)(2,1)}) %reduce-scatter.2.cloned.1.call-update) | async-done | bytes 524304 | tf_op jit(solution)/shard_map/reduce_scatter | solution.py:47
  204.1 1.2 copy.20
  205.3 13.6 %all_to_all.17 = bf16[4,2,256,128]{2,3,1,0:T(8,128)(2,1)S(1)} all-to-all(bf16[4,2,256,128]{2,3,1,0:T(8,128)(2,1)S(1)} %copy.20), channel_id=1, replica_groups=mesh['sg'=4,'sr'=4,'my'=8,'mx'=4] {'mx'}, dimensions={0} | all-to-all | bytes 1048576 | tf_op jit(solution)/shard_map/all_to_all | solution.py:49
  218.9 0.1 convert_reduce_fusion
  219.0 0.0 copy-done.1
  219.0 0.0 copy-done.2
  219.0 2.3 collective-permute-start.4
  221.3 0.0 collective-permute-start.3
  221.3 1.9 collective-permute-done.4
  223.2 3.0 %collective-permute-done.3 = bf16[1,128,256]{2,1,0:T(8,128)(2,1)S(1)} collective-permute-done((bf16[1,128,256]{2,1,0:T(8,128)(2,1)S(1)}, bf16[1,128,256]{2,1,0:T(8,128)(2,1)S(1)}, u32[]{:S(2)}, u32[]{:S(2)}) %collective-permute-start.3) | collective-permute-done | bytes 65568 | tf_op jit(solution)/shard_map/ppermute | solution.py:16
  226.2 0.6 copy.32
  226.8 0.6 copy.33
  (11 shorter events, 0.2 us)
Async XLA Ops:
  7.2 15.5 %copy-start.3 = (s32[1,2,2,2]{3,2,1,0:T(2,128)S(1)}, s32[1,2,2,2]{3,2,1,0:T(2,128)}, u32[]{:S(2)}) copy-start(s32[1,2,2,2]{3,2,1,0:T(2,128)} %param.9) | copy-start | bytes 100
  7.2 96.7 %all-gather.2.cloned.1.call-start = ((), (), s32[]{:S(2)}) async-start(), calls=%async_computation.4 | async-start | bytes 7077888 | tf_op jit(solution)/shard_map/all_gather | solution.py:80
  22.6 181.5 %reduce-scatter.2.cloned.1.call-start = ((), (), s32[]{:S(2)}) async-start(), calls=%async_computation.5 | async-start | bytes 4718592 | tf_op jit(solution)/shard_map/reduce_scatter | solution.py:47
  103.9 2.2 slice-start
  103.9 2.9 %copy-start = (bf16[8192,128]{1,0:T(8,128)(2,1)S(1)}, bf16[8192,128]{1,0:T(8,128)(2,1)}, u32[]{:S(2)}) copy-start(bf16[8192,128]{1,0:T(8,128)(2,1)} %get-tuple-element.54) | copy-start | bytes 6291460
  108.1 12.3 %collective-permute-start.2 = (bf16[256,256]{1,0:T(8,128)(2,1)S(1)}, bf16[256,256]{1,0:T(8,128)(2,1)S(1)}, u32[]{:S(2)}, u32[]{:S(2)}) collective-permute-start(bf16[256,256]{1,0:T(8,128)(2,1)S(1)} %get-tuple-element.39), channel_id=1, source_target_pairs={{384,0},{385,1},{386,2},{387,3},{388,4},{389,5},{390,6},{391,7},{3... | collective-permute-start | bytes 393224 | tf_op jit(solution)/shard_map/ppermute | solution.py:110
  109.4 11.0 %collective-permute-start.1 = (bf16[256,256]{1,0:T(8,128)(2,1)S(1)}, bf16[256,256]{1,0:T(8,128)(2,1)S(1)}, u32[]{:S(2)}, u32[]{:S(2)}) collective-permute-start(bf16[256,256]{1,0:T(8,128)(2,1)S(1)} %get-tuple-element.39), channel_id=1, source_target_pairs={{384,128},{385,129},{386,130},{387,131},{388,132},{389,133},{390,1... | collective-permute-start | bytes 393224 | tf_op jit(solution)/shard_map/ppermute | solution.py:110
  110.1 10.3 %collective-permute-start = (bf16[256,256]{1,0:T(8,128)(2,1)S(1)}, bf16[256,256]{1,0:T(8,128)(2,1)S(1)}, u32[]{:S(2)}, u32[]{:S(2)}) collective-permute-start(bf16[256,256]{1,0:T(8,128)(2,1)S(1)} %get-tuple-element.39), channel_id=1, source_target_pairs={{384,256},{385,257},{386,258},{387,259},{388,260},{389,261},{390,2... | collective-permute-start | bytes 393224 | tf_op jit(solution)/shard_map/ppermute | solution.py:110
  192.7 26.3 %copy-start.1 = (bf16[1,2,128,256]{3,2,1,0:T(8,128)(2,1)S(1)}, bf16[1,2,128,256]{3,2,1,0:T(8,128)(2,1)}, u32[]{:S(2)}) copy-start(bf16[1,2,128,256]{3,2,1,0:T(8,128)(2,1)} %param.6) | copy-start | bytes 393220
  192.7 26.3 %copy-start.2 = (bf16[1,128,256]{2,1,0:T(8,128)(2,1)S(1)}, bf16[1,128,256]{2,1,0:T(8,128)(2,1)}, u32[]{:S(2)}) copy-start(bf16[1,128,256]{2,1,0:T(8,128)(2,1)} %param.7) | copy-start | bytes 196612
  219.0 4.2 %collective-permute-start.4 = (bf16[1,128,256]{2,1,0:T(8,128)(2,1)S(1)}, bf16[1,128,256]{2,1,0:T(8,128)(2,1)S(1)}, u32[]{:S(2)}, u32[]{:S(2)}) collective-permute-start(bf16[1,128,256]{2,1,0:T(8,128)(2,1)S(1)} %get-tuple-element.56), channel_id=1, source_target_pairs={{0,480},{32,0},{64,32},{96,64},{128,96},{160,128},{192,160},{224,1... | collective-permute-start | bytes 196616 | tf_op jit(solution)/shard_map/ppermute | solution.py:16
  221.3 4.9 %collective-permute-start.3 = (bf16[1,128,256]{2,1,0:T(8,128)(2,1)S(1)}, bf16[1,128,256]{2,1,0:T(8,128)(2,1)S(1)}, u32[]{:S(2)}, u32[]{:S(2)}) collective-permute-start(bf16[1,128,256]{2,1,0:T(8,128)(2,1)S(1)} %get-tuple-element.57), channel_id=1, source_target_pairs={{0,32},{32,64},{64,96},{96,128},{128,160},{160,192},{192,224},{224... | collective-permute-start | bytes 196616 | tf_op jit(solution)/shard_map/ppermute | solution.py:16
Sparse Core Ops, SparseCore 0:
  22.7 81.0 all-gather.1
  148.7 55.3 reduce-scatter.1
where the time goes:
time: 235 us; the launch traced here: 234 us
  waiting for transfers between devices  99.2 us (42%)
  blocking collectives  81 us (34%)
  local copies, waits for them, and re-layouts  17.2 us (7%)
  between operations  14.3 us (6%)
  matrix products  11.3 us (5%)
  other arithmetic  6.31 us (3%)
  starting transfers between devices  4.98 us (2%)
    all_gather x1, waiting for transfers between devices, per_device(): gathered = lax.all_gather(gathered, stage, axis=2, tiled=True)  77.2 us
    all_to_all x1, blocking collectives, segment_sum(): moved = lax.all_to_all(parts, axis, 0, 0, tiled=True)  21.9 us
    all_to_all x1, blocking collectives, segment_sum(): return lax.all_to_all(spread, axis, 0, 0, tiled=True).reshape(contrib.shape)  20 us
    all_gather x1, blocking collectives, per_device(): gathered = lax.all_gather(gathered, stage, axis=2, tiled=True)  14.4 us
    all_to_all x1, blocking collectives, head_sum(): moved = lax.all_to_all(partial, axis[1], 0, 0, tiled=True)  13.6 us
    all_gather x1, blocking collectives, per_device(): lax.all_gather(piece, 'sr', axis=0, tiled=True)  11.1 us
    reduce_scatter x1, waiting for transfers between devices, head_sum(): lax.psum_scatter(parts, axis[0], scatter_dimension=0, tiled=True)[0]  10.4 us
    ppermute x3, waiting for transfers between devices, per_device(): arrived = lax.ppermute(encoded, 'sg', [(last_group, target)])  6.71 us
  transfers between devices with their start and end apart: 7, of which 5 were waited for; matrix products, arithmetic and copies ran while one was open for 4% of the time, Pallas kernels for 0%

commit v1 on v0

--- a/solution.py
+++ b/solution.py
@@ -77,7 +77,18 @@
     local_carry = carry[0]
     gathered = jnp.concatenate([local_rows, local_carry[None]], axis=0)
     for stage in stages:
-        gathered = lax.all_gather(gathered, stage, axis=2, tiled=True)
+
+        def find_streams(xin, shard_axis):
+            trail = []
+            for _ in range(lax.axis_size(shard_axis)):
+                trail.append(xin)
+            before = jnp.concatenate(
+                lax.all_to_all(jnp.stack(trail), axis_name=shard_axis, split_axis=0, concat_axis=0),
+                axis=2,
+            )
+            return before
+
+        gathered = find_streams(gathered, stage)
     full_rows, full_carry = (gathered[:2], gathered[2])
     tokens = local_rows.shape[1]
     width = full_rows.shape[2]

time: 235 us -> 331 us (1.41)
  waiting for transfers between devices: 99.2 us -> 161 us
  local copies, waits for them, and re-layouts: 17.2 us -> 41.1 us
  starting transfers between devices: 4.98 us -> 12.4 us
    all_to_all x0 -> x1, waiting for transfers between devices: none -> 127 us  [find_streams(): lax.all_to_all(jnp.stack(trail), axis_name=shard_axis, split_axis=0, conc...]
    all_gather x1 -> x0, waiting for transfers between devices: 77.2 us -> none  [per_device(): gathered = lax.all_gather(gathered, stage, axis=2, tiled=True)]
    all_to_all x0 -> x1, blocking collectives: none -> 16.4 us  [find_streams(): lax.all_to_all(jnp.stack(trail), axis_name=shard_axis, split_axis=0, conc...]
    all_gather x1 -> x0, blocking collectives: 14.4 us -> none  [per_device(): gathered = lax.all_gather(gathered, stage, axis=2, tiled=True)]
    another operation x1 -> x5, local copies, waits for them, and re-layouts: 0.01 us -> 10.2 us
    all_to_all x0 -> x2, local copies, waits for them, and re-layouts: none -> 8.98 us  [find_streams(): lax.all_to_all(jnp.stack(trail), axis_name=shard_axis, split_axis=0, conc...]
    reduce_scatter x1, waiting for transfers between devices: 10.4 us -> 18.9 us  [head_sum(): lax.psum_scatter(parts, axis[0], scatter_dimension=0, tiled=True)[0]]
    all_to_all x0 -> x1, starting transfers between devices: none -> 7.45 us  [find_streams(): lax.all_to_all(jnp.stack(trail), axis_name=shard_axis, split_axis=0, conc...]
  transfers between devices with their start and end apart: 7 -> 7, of which waited for: 5 -> 5; matrix products, arithmetic and copies ran while one was open for 4% -> 3% of each run, Pallas kernels for 0% -> 0%
where the time goes in v1:
time: 331 us; the launch traced here: 330 us
  waiting for transfers between devices  161 us (49%)
  blocking collectives  81.2 us (25%)
  local copies, waits for them, and re-layouts  41.1 us (12%)
  between operations  14.3 us (4%)
  matrix products  13.5 us (4%)
  starting transfers between devices  12.4 us (4%)
  other arithmetic  6.31 us (2%)
    all_to_all x1, waiting for transfers between devices, find_streams(): lax.all_to_all(jnp.stack(trail), axis_name=shard_axis, split_axis=0, conc...  127 us
    all_to_all x1, blocking collectives, segment_sum(): moved = lax.all_to_all(parts, axis, 0, 0, tiled=True)  21.1 us
    all_to_all x1, blocking collectives, segment_sum(): return lax.all_to_all(spread, axis, 0, 0, tiled=True).reshape(contrib.shape)  20 us
    reduce_scatter x1, waiting for transfers between devices, head_sum(): lax.psum_scatter(parts, axis[0], scatter_dimension=0, tiled=True)[0]  18.9 us
    all_to_all x1, blocking collectives, find_streams(): lax.all_to_all(jnp.stack(trail), axis_name=shard_axis, split_axis=0, conc...  16.4 us
    all_to_all x1, blocking collectives, head_sum(): moved = lax.all_to_all(partial, axis[1], 0, 0, tiled=True)  13.6 us
    ppermute x3, waiting for transfers between devices, per_device(): arrived = lax.ppermute(encoded, 'sg', [(last_group, target)])  10.5 us
    all_gather x1, blocking collectives, per_device(): lax.all_gather(piece, 'sr', axis=0, tiled=True)  10 us
  transfers between devices with their start and end apart: 7, of which 5 were waited for; matrix products, arithmetic and copies ran while one was open for 3% of the time, Pallas kernels for 0%

profile of v1, /device:TPU:24, one launch (start us, length us, event | category | flops | bytes accessed | tf_op | source)
XLA Modules:
  0.0 329.7 jit_solution(4014596026994226884)
XLA Ops:
  7.2 1.0 pad_maximum_fusion.2
  8.1 0.1 stack.19
  8.2 16.4 %all_to_all.25 = bf16[4,3,128,256]{3,2,1,0:T(8,128)(2,1)S(1)} all-to-all(bf16[4,3,128,256]{3,2,1,0:T(8,128)(2,1)S(1)} %stack.19), channel_id=1, replica_groups=mesh['sg'=4,'sr'=4,'my'=8,'mx'=4] {'mx'}, dimensions={0} | all-to-all | bytes 1572864 | tf_op jit(solution)/shard_map/all_to_all | solution.py:86
  24.6 0.4 copy.22
  25.0 0.3 copy.23
  25.3 3.5 %stack.20 = bf16[8,3,128,1024]{3,2,1,0:T(8,128)(2,1)} broadcast(bf16[3,128,1024]{2,1,0:T(8,128)(2,1)S(1)} %copy.23), dimensions={1,2,3} | broadcast | bytes 7077888 | tf_op jit(solution)/shard_map/stack | solution.py:86
  28.8 7.5 %all-to-all-start.1 = ((bf16[8,3,128,1024]{3,2,1,0:T(8,128)(2,1)}), bf16[8,3,128,1024]{3,2,1,0:T(8,128)(2,1)}, u32[]{:S(2)}, u32[]{:S(2)}) async-start(bf16[8,3,128,1024]{3,2,1,0:T(8,128)(2,1)} %stack.20), calls=%async_computation.1 | async-start | bytes 12582912 | tf_op jit(solution)/shard_map/all_to_all | solution.py:86
  36.2 0.0 reduce-scatter.2.cloned.1.call-start
  36.2 0.0 copy-done.3
  36.2 0.1 reshape.155
  36.3 0.1 reshape.163
  36.4 3.8 %slice_bitcast_fusion = (bf16[8192,128]{1,0:T(8,128)(2,1)}, bf16[8192,128]{1,0:T(8,128)(2,1)S(1)}) fusion(bf16[1,2,8192,128]{3,2,1,0:T(8,128)(2,1)} %param.8), kind=kLoop, calls=%fused_computation.13 | loop fusion | bytes 8388608 | tf_op jit(solution)/shard_map/squeeze | solution.py:97
  40.3 126.7 %all-to-all-done.1 = bf16[8,3,128,1024]{3,2,1,0:T(8,128)(2,1)} async-done(((bf16[8,3,128,1024]{3,2,1,0:T(8,128)(2,1)}), bf16[8,3,128,1024]{3,2,1,0:T(8,128)(2,1)}, u32[]{:S(2)}, u32[]{:S(2)}) %all-to-all-start.1) | async-done | bytes 6291488 | tf_op jit(solution)/shard_map/all_to_all | solution.py:86
  166.9 8.6 %copy.24 = bf16[8,3,128,1024]{2,3,0,1:T(8,128)(2,1)} copy(bf16[8,3,128,1024]{3,2,1,0:T(8,128)(2,1)} %all-to-all-done.1) | data formatting | bytes 12582912 | tf_op jit(solution)/shard_map/all_to_all | solution.py:86
  175.6 3.0 slice.80
  178.6 4.6 %slice.76 = bf16[2,128,8,1024]{1,3,2,0:T(8,128)(2,1)} slice(bf16[3,128,8,1024]{1,3,2,0:T(8,128)(2,1)} %bitcast.86), slice={[0:2], [0:128], [0:8], [0:1024]} | slice | bytes 8388608 | tf_op jit(solution)/shard_map/slice | solution.py:92
  183.2 9.8 %conditional.1 = (bf16[256,256]{1,0:T(8,128)(2,1)S(1)}, bf16[2,64,128]{2,1,0:T(8,128)(2,1)S(1)}, bf16[2,64,128]{2,1,0:T(8,128)(2,1)S(1)}) conditional(s32[]{:T(128)} %convert_element_type.64, (bf16[2,128,8192]{1,2,0:T(8,128)(2,1)}, bf16[8192,128]{1,0:T(8,128)(2,1)S(1)}) %tuple.45, (bf16[2,128,8192]{1,2,0:T(8,128)(2,1)}, ...), branch_computations={%region_0.0_spmd, %region_1.0_spmd} | conditional | flops 1074069504 | bytes 38469688 | solution.py:116
  183.2 6.3 %copy.25 = bf16[2,128,8192]{2,1,0:T(8,128)(2,1)} copy(bf16[2,128,8192]{1,2,0:T(8,128)(2,1)} %get-tuple-element.55) | data formatting | bytes 8388608 | tf_op jit(solution)/shard_map
  189.5 3.4 %convolution_convert_fusion = bf16[256,128]{1,0:T(8,128)(2,1)S(1)} fusion(bf16[256,8192]{1,0:T(8,128)(2,1)} %bitcast.87, bf16[8192,128]{1,0:T(8,128)(2,1)S(1)} %get-tuple-element.26), kind=kOutput, calls=%fused_computation.2 | convolution fusion | flops 536903680 | bytes 6356992 | tf_op jit(solution)/shard_map/cond/branch_0_fun/dot_general | solution.py:111
  193.0 1.3 collective-permute-start.2
  194.3 0.7 collective-permute-start.1
  194.9 0.7 collective-permute-start
  195.6 3.0 convolution_convert_fusion.5
  198.6 10.5 %collective-permute-done.2 = bf16[256,256]{1,0:T(8,128)(2,1)S(1)} collective-permute-done((bf16[256,256]{1,0:T(8,128)(2,1)S(1)}, bf16[256,256]{1,0:T(8,128)(2,1)S(1)}, u32[]{:S(2)}, u32[]{:S(2)}) %collective-permute-start.2) | collective-permute-done | bytes 131104 | tf_op jit(solution)/shard_map/ppermute | solution.py:121
  209.1 0.0 collective-permute-done.1
  209.1 0.0 collective-permute-done
  209.1 10.0 %all_gather.3 = bf16[1024,256]{1,0:T(8,128)(2,1)S(1)} all-gather(bf16[256,256]{1,0:T(8,128)(2,1)S(1)} %select_select_fusion), channel_id=1, replica_groups=mesh['sg'=4,'sr'=4,'my'=8,'mx'=4] {'sr'}, dimensions={0}, use_global_device_ids=true | all-gather | bytes 655360 | tf_op jit(solution)/shard_map/all_gather | solution.py:123
  219.2 0.6 gather_fusion.1
  219.7 0.6 gather_fusion
  220.3 0.2 convolution_multiply_fusion.2
  220.5 0.2 fusion.31
  220.7 0.3 convolution_convert_fusion.6
  221.0 0.2 convolution_multiply_fusion.1
  221.2 0.4 fusion.30
  221.5 0.3 multiply_reduce_fusion
  221.8 0.3 fusion.10
  222.1 2.3 fusion.3
  224.5 2.5 copy.35
  226.9 2.3 fusion.2
  229.2 2.5 copy.34
  231.7 4.5 %maximum_bitcast_fusion = bf16[8,4,2,256,128]{4,3,2,1,0:T(8,128)(2,1)} fusion(bf16[1,8,4,256,128]{4,3,0,2,1:T(8,128)(2,1)} %bitcast.88, bf16[1,8,4,256,128]{4,3,0,2,1:T(8,128)(2,1)} %bitcast.89), kind=kLoop, calls=%fused_computation.12 | loop fusion | flops 2097152 | bytes 8388608 | tf_op jit(solution)/shard_map/transpose | solution.py:44
  236.2 0.0 reduce-scatter.2.cloned.1.call-update
  236.3 0.1 copy.29
  236.3 0.3 fusion.21
  236.7 0.4 convolution_multiply_fusion
  237.1 0.1 reshape.151
  237.2 0.5 copy.30
  237.7 0.5 fusion.5
  238.2 0.1 copy.31
  238.3 21.1 %all_to_all.26 = bf16[16,64,256]{2,1,0:T(8,128)(2,1)S(1)} all-to-all(bf16[16,64,256]{2,1,0:T(8,128)(2,1)S(1)} %bitcast.94), channel_id=1, replica_groups=mesh['sg'=4,'sr'=4,'my'=8,'mx'=4] {'sg','sr'}, dimensions={0} | all-to-all | bytes 1048576 | tf_op jit(solution)/shard_map/all_to_all | solution.py:62
  259.4 0.1 reduce_sum.51
  259.6 20.0 %all_to_all.27 = bf16[16,64,256]{2,1,0:T(8,128)(2,1)S(1)} all-to-all(bf16[16,64,256]{2,1,0:T(8,128)(2,1)S(1)} %broadcast_in_dim.5), channel_id=1, replica_groups=mesh['sg'=4,'sr'=4,'my'=8,'mx'=4] {'sg','sr'}, dimensions={0} | all-to-all | bytes 1048576 | tf_op jit(solution)/shard_map/all_to_all | solution.py:65
  279.6 0.9 reshape_reshape.7
  280.5 18.9 %reduce-scatter.2.cloned.1.call-done = bf16[1,4,2,256,128]{4,3,2,1,0:T(8,128)(2,1)} async-done(((bf16[8,4,2,256,128]{4,3,2,1,0:T(8,128)(2,1)}), bf16[1,4,2,256,128]{4,3,2,1,0:T(8,128)(2,1)}) %reduce-scatter.2.cloned.1.call-update) | async-done | bytes 524304 | tf_op jit(solution)/shard_map/reduce_scatter | solution.py:47
  299.4 1.2 copy.32
  300.7 13.6 %all_to_all.28 = bf16[4,2,256,128]{2,3,1,0:T(8,128)(2,1)S(1)} all-to-all(bf16[4,2,256,128]{2,3,1,0:T(8,128)(2,1)S(1)} %copy.32), channel_id=1, replica_groups=mesh['sg'=4,'sr'=4,'my'=8,'mx'=4] {'mx'}, dimensions={0} | all-to-all | bytes 1048576 | tf_op jit(solution)/shard_map/all_to_all | solution.py:49
  314.3 0.1 convert_reduce_fusion
  314.3 0.0 copy-done.1
  314.4 2.3 collective-permute-start.4
  316.7 0.0 collective-permute-start.3
  316.7 1.9 collective-permute-done.4
  318.6 3.0 collective-permute-done.3
  321.6 0.6 copy.44
  322.2 0.6 copy.45
  (14 shorter events, 0.2 us)
Async XLA Ops:
  28.8 7.5 %copy-start.3 = (s32[1,2,2,2]{3,2,1,0:T(2,128)S(1)}, s32[1,2,2,2]{3,2,1,0:T(2,128)}, u32[]{:S(2)}) copy-start(s32[1,2,2,2]{3,2,1,0:T(2,128)} %param.9) | copy-start | bytes 100
  28.8 138.2 %all-to-all-start.1 = ((bf16[8,3,128,1024]{3,2,1,0:T(8,128)(2,1)}), bf16[8,3,128,1024]{3,2,1,0:T(8,128)(2,1)}, u32[]{:S(2)}, u32[]{:S(2)}) async-start(bf16[8,3,128,1024]{3,2,1,0:T(8,128)(2,1)} %stack.20), calls=%async_computation.1 | async-start | bytes 12582912 | tf_op jit(solution)/shard_map/all_to_all | solution.py:86
  36.2 263.2 %reduce-scatter.2.cloned.1.call-start = ((), (), s32[]{:S(2)}) async-start(), calls=%async_computation.6 | async-start | bytes 4718592 | tf_op jit(solution)/shard_map/reduce_scatter | solution.py:47
  193.0 16.1 %collective-permute-start.2 = (bf16[256,256]{1,0:T(8,128)(2,1)S(1)}, bf16[256,256]{1,0:T(8,128)(2,1)S(1)}, u32[]{:S(2)}, u32[]{:S(2)}) collective-permute-start(bf16[256,256]{1,0:T(8,128)(2,1)S(1)} %get-tuple-element.39), channel_id=1, source_target_pairs={{384,0},{385,1},{386,2},{387,3},{388,4},{389,5},{390,6},{391,7},{3... | collective-permute-start | bytes 393224 | tf_op jit(solution)/shard_map/ppermute | solution.py:121
  194.3 14.8 %collective-permute-start.1 = (bf16[256,256]{1,0:T(8,128)(2,1)S(1)}, bf16[256,256]{1,0:T(8,128)(2,1)S(1)}, u32[]{:S(2)}, u32[]{:S(2)}) collective-permute-start(bf16[256,256]{1,0:T(8,128)(2,1)S(1)} %get-tuple-element.39), channel_id=1, source_target_pairs={{384,128},{385,129},{386,130},{387,131},{388,132},{389,133},{390,1... | collective-permute-start | bytes 393224 | tf_op jit(solution)/shard_map/ppermute | solution.py:121
  194.9 14.2 %collective-permute-start = (bf16[256,256]{1,0:T(8,128)(2,1)S(1)}, bf16[256,256]{1,0:T(8,128)(2,1)S(1)}, u32[]{:S(2)}, u32[]{:S(2)}) collective-permute-start(bf16[256,256]{1,0:T(8,128)(2,1)S(1)} %get-tuple-element.39), channel_id=1, source_target_pairs={{384,256},{385,257},{386,258},{387,259},{388,260},{389,261},{390,2... | collective-permute-start | bytes 393224 | tf_op jit(solution)/shard_map/ppermute | solution.py:121
  279.6 34.8 %copy-start.1 = (bf16[1,2,128,256]{3,2,1,0:T(8,128)(2,1)S(1)}, bf16[1,2,128,256]{3,2,1,0:T(8,128)(2,1)}, u32[]{:S(2)}) copy-start(bf16[1,2,128,256]{3,2,1,0:T(8,128)(2,1)} %param.6) | copy-start | bytes 393220
  279.6 34.8 %copy-start.2 = (bf16[1,128,256]{2,1,0:T(8,128)(2,1)S(1)}, bf16[1,128,256]{2,1,0:T(8,128)(2,1)}, u32[]{:S(2)}) copy-start(bf16[1,128,256]{2,1,0:T(8,128)(2,1)} %param.7) | copy-start | bytes 196612
  314.4 4.2 %collective-permute-start.4 = (bf16[1,128,256]{2,1,0:T(8,128)(2,1)S(1)}, bf16[1,128,256]{2,1,0:T(8,128)(2,1)S(1)}, u32[]{:S(2)}, u32[]{:S(2)}) collective-permute-start(bf16[1,128,256]{2,1,0:T(8,128)(2,1)S(1)} %get-tuple-element.64), channel_id=1, source_target_pairs={{0,480},{32,0},{64,32},{96,64},{128,96},{160,128},{192,160},{224,1... | collective-permute-start | bytes 196616 | tf_op jit(solution)/shard_map/ppermute | solution.py:16
  316.7 4.9 %collective-permute-start.3 = (bf16[1,128,256]{2,1,0:T(8,128)(2,1)S(1)}, bf16[1,128,256]{2,1,0:T(8,128)(2,1)S(1)}, u32[]{:S(2)}, u32[]{:S(2)}) collective-permute-start(bf16[1,128,256]{2,1,0:T(8,128)(2,1)S(1)} %get-tuple-element.65), channel_id=1, source_target_pairs={{0,32},{32,64},{64,96},{96,128},{128,160},{160,192},{192,224},{224... | collective-permute-start | bytes 196616 | tf_op jit(solution)/shard_map/ppermute | solution.py:16
Sparse Core Ops, SparseCore 0:
  236.4 63.0 reduce-scatter.1
